TPU v7x, 256 devices: a whole 4x4x8 slice. The times are simulated.
256 devices in a mesh: seq: 32 (over x, y, z_hi), tp: 8 (over z_lo, core).
Axes of the slice: x: 4, y: 4, z: 8 (z_hi: 2, z_lo: 4; z = z_hi * 4 + z_lo), core: 2. Of those that a mesh axis runs over, the one named last changes fastest.
Arguments:
- prefill_tokens: bfloat16 [8192, 4608], P('seq'), may hold values from -6 to 6
- decode_tokens: bfloat16 [64, 4608], replicated, may hold values from -6 to 6
- norm_gain: float32 [4608], replicated, may hold values from 0.1 to 1.9
- w_query: bfloat16 [4608, 4096], P('seq', 'tp'), may hold values from -2.1213203 to 2.1213203
- w_key: bfloat16 [4608, 2048], P('seq', 'tp'), may hold values from -0.09375 to 0.09375
- w_value: bfloat16 [4608, 2048], P('seq', 'tp'), may hold values from -0.09375 to 0.09375
- w_output: bfloat16 [4096, 4608], P('seq', 'tp'), may hold values from -0.09375 to 0.09375
- prefill_lengths: int32 [6], replicated, may hold values from 1 to 6144, 8192 in all
- context_lengths: int32 [2], replicated, may hold values from 2048 to 8192, as said below
- tail_lengths: int32 [32], replicated, may hold values from 1 to 256, as said below
- tail_slots: int32 [32], replicated, may hold values from 0 to 63, as said below
- cache_keys: bfloat16 [2, 8192, 2048], P(None, 'seq', 'tp'), may hold values from -6 to 6
- cache_values: bfloat16 [2, 8192, 2048], P(None, 'seq', 'tp'), may hold values from -6 to 6
- tail_keys: bfloat16 [64, 256, 2048], P('seq', None, 'tp'), may hold values from -6 to 6
- tail_values: bfloat16 [64, 256, 2048], P('seq', None, 'tp'), may hold values from -6 to 6
Outputs:
- prefill_out: bfloat16 [8192, 4608], P('seq', 'tp')
- decode_out: bfloat16 [64, 4608], P('seq', 'tp')
Inputs may be any that keep to these rules, and one draw needn't show every extreme that they name: `prefill_lengths`: the prompts fill all 8192 prefill tokens; the longest has exactly 6144. `context_lengths`: some prompt has exactly 8192 cached positions. `tail_lengths`: some sample has exactly 256 tail positions. `tail_slots`: distinct slot numbers; slot q lies with seq index q // 2; in every draw all slots of some seq index are used.
All inputs are finite; a program needn't handle non-finite values.
Results may differ from a plain program's by a relative error of at most 0.019.
Values may be sent and summed in bfloat16 or wider, within the bound.
No kernel may reach another device: no remote copies, remote signals or barrier semaphores. Data moves between devices by JAX's collectives and lax.ppermute only.
A program may use at most 128 MiB of HBM per device.

v0:
```python
import math
import jax
import jax.numpy as jnp
from jax import lax
from jax.sharding import PartitionSpec as P

HEAD = 128
SAMPLES = 16
NEW = 2
SOFTCAP = 50.0
QUERY_SCALE = 144.0 ** (-0.5)
NORM_EPSILON = 1e-06
ROPE_BASE = 10000.0


def combined_all(shard, axis, combine):
    everything = jax.tree.map(
        lambda part, kind: lax.all_gather(part.astype(kind), axis),
        shard,
        jax.tree.map(lambda a: jnp.bfloat16 if a.dtype == jnp.float32 else a.dtype, shard),
    )

    def take(k):
        return jax.tree.map(lambda part, own: part[k].astype(own.dtype), everything, shard)

    return lax.fori_loop(
        1, lax.axis_size(axis), lambda k, so_far: combine(so_far, take(k)), take(0)
    )


def rms_norm(inputs, norm_gain):
    values = inputs.astype(jnp.float32)
    mean_sq = jnp.mean(values * values, axis=-1, keepdims=True)
    return (values * lax.rsqrt(mean_sq + NORM_EPSILON) * norm_gain).astype(jnp.bfloat16)


def rotate(values, positions):
    half_size = values.shape[-1] // 2
    exponent = jnp.arange(half_size, dtype=jnp.float32) * (2.0 / values.shape[-1])
    frequency = ROPE_BASE ** (-exponent)
    angles = positions.astype(jnp.float32)[:, None] * frequency[None, :]
    cosine = jnp.cos(angles)[:, None, :]
    sine_part = jnp.sin(angles)[:, None, :]
    lower_half = values[..., :half_size]
    upper_half = values[..., half_size:]
    return jnp.concatenate(
        [
            lower_half * cosine - upper_half * sine_part,
            upper_half * cosine + lower_half * sine_part,
        ],
        axis=-1,
    )


def soft_cap(scores):
    return SOFTCAP * jnp.tanh(scores / SOFTCAP)


def prefill_positions(prefill_lengths, token_index):
    prompt_ends = jnp.cumsum(prefill_lengths)
    passed = token_index[:, None] >= prompt_ends[None, :]
    segment = jnp.sum(passed.astype(jnp.int32), axis=1)
    start_at = jnp.sum(jnp.where(passed, prefill_lengths[None, :], 0), axis=1)
    return (segment, token_index - start_at)


def lookup(table, indices):
    entries = jnp.arange(table.shape[0], dtype=jnp.int32)
    return jnp.sum(jnp.where(indices[:, None] == entries[None, :], table[None, :], 0), axis=1)


def combine(earlier, later):
    return (earlier[0] + later[0], earlier[1] + later[1])


def partial_softmax(scores, allowed, value_block, form):
    weights = jnp.where(allowed, jnp.exp(scores), 0.0)
    total_sum = jnp.sum(weights, axis=-1)
    mixed_out = jnp.einsum(
        form, weights.astype(jnp.bfloat16), value_block, preferred_element_type=jnp.float32
    )
    return (total_sum, mixed_out)


def shards(
    prefill_tokens,
    decode_tokens,
    norm_gain,
    w_query,
    w_key,
    w_value,
    w_output,
    prefill_lengths,
    context_lengths,
    tail_lengths,
    tail_slots,
    cache_keys,
    cache_values,
    tail_keys,
    tail_values,
):
    seq_count = lax.axis_size("seq")
    seq_index = lax.axis_index("seq")
    pf_rows = prefill_tokens.shape[0]
    dec_total = decode_tokens.shape[0]
    dec_rows = dec_total // seq_count
    q_heads = w_query.shape[1] // HEAD
    kv_heads = w_key.shape[1] // HEAD
    group_size = q_heads // kv_heads
    token_index = seq_index * pf_rows + jnp.arange(pf_rows, dtype=jnp.int32)
    query_seg, pf_positions = prefill_positions(prefill_lengths, token_index)
    row_ids = jnp.arange(dec_total, dtype=jnp.int32)
    sample_ids = row_ids // NEW
    dec_positions = (
        lookup(context_lengths, sample_ids // SAMPLES)
        + lookup(tail_lengths, sample_ids)
        + row_ids % NEW
    )
    positions = jnp.concatenate([pf_positions, dec_positions], axis=0)
    normed = rms_norm(jnp.concatenate([prefill_tokens, decode_tokens], axis=0), norm_gain)
    row_total = normed.shape[0]
    pieces = (
        lax.all_gather(w_query, "seq", axis=0, tiled=True),
        lax.all_gather(w_key, "seq", axis=0, tiled=True),
        lax.all_gather(w_value, "seq", axis=0, tiled=True),
    )
    columns = normed
    query_all, key_all, value_all = tuple(
        (jnp.dot(columns, piece_part, preferred_element_type=jnp.float32) for piece_part in pieces)
    )
    query_all = (
        rotate(query_all.reshape(row_total, q_heads, HEAD), positions) * QUERY_SCALE
    ).astype(jnp.bfloat16)
    key_all = (
        rotate(key_all.reshape(row_total, kv_heads, HEAD), positions)
        .astype(jnp.bfloat16)
        .reshape(row_total, -1)
    )
    value_all = value_all.astype(jnp.bfloat16)
    pf_query = query_all[:pf_rows].reshape(pf_rows, kv_heads, group_size, HEAD)
    pf_key = key_all[:pf_rows]
    pf_value = value_all[:pf_rows]
    query_last = token_index[pf_rows - 1]
    prompt_first = token_index[0] - pf_positions[0]
    start_state = (
        jnp.zeros((pf_rows, kv_heads, group_size), jnp.float32),
        jnp.zeros((pf_rows, kv_heads, group_size, HEAD), jnp.float32),
    )
    key_piece = lax.all_gather(pf_key, "seq", axis=0, tiled=True)
    value_piece = lax.all_gather(pf_value, "seq", axis=0, tiled=True)
    piece_len = key_piece.shape[0]
    block_len = math.gcd(512, piece_len)

    def one_block(block_step, carry_state):
        begin = block_step * block_len
        key_block = lax.dynamic_slice_in_dim(
            key_piece, block_step * block_len, block_len, 0
        ).reshape(block_len, kv_heads, HEAD)
        value_block = lax.dynamic_slice_in_dim(
            value_piece, block_step * block_len, block_len, 0
        ).reshape(block_len, kv_heads, HEAD)

        def compute(state_in):
            key_index = begin + jnp.arange(block_len, dtype=jnp.int32)
            key_seg, unused_pos = prefill_positions(prefill_lengths, key_index)
            allowed = (query_seg[:, None] == key_seg[None, :]) & (
                key_index[None, :] <= token_index[:, None]
            )
            scores = soft_cap(
                jnp.einsum(
                    "qgjd,kgd->qgjk", pf_query, key_block, preferred_element_type=jnp.float32
                )
            )
            weights = jnp.where(allowed[:, None, None, :], jnp.exp(scores), 0.0)
            total_sum = state_in[0] + jnp.sum(weights, axis=-1)
            mixed_out = state_in[1] + jnp.einsum(
                "qgjk,kgd->qgjd",
                weights.astype(jnp.bfloat16),
                value_block,
                preferred_element_type=jnp.float32,
            )
            return (total_sum, mixed_out)

        is_live = (begin <= query_last) & (begin + block_len > prompt_first)
        return lax.cond(is_live, compute, lambda state_in: state_in, carry_state)

    pf_state = lax.fori_loop(0, piece_len // block_len, one_block, start_state)
    pf_attn = (
        (pf_state[1] / pf_state[0][..., None]).astype(jnp.bfloat16).reshape(pf_rows, q_heads * HEAD)
    )
    dec_query = query_all[pf_rows:]
    dec_key = key_all[pf_rows:]
    dec_value = value_all[pf_rows:]
    prompt_count = cache_keys.shape[0]
    ctx_rows = cache_keys.shape[1]
    prompt_queries = dec_query.reshape(prompt_count, SAMPLES * NEW, kv_heads, group_size, HEAD)
    cache_k = cache_keys.reshape(prompt_count, ctx_rows, kv_heads, HEAD)
    cache_v = cache_values.reshape(prompt_count, ctx_rows, kv_heads, HEAD)
    cache_pos = seq_index * ctx_rows + jnp.arange(ctx_rows, dtype=jnp.int32)
    cache_allowed = (cache_pos[None, :] < context_lengths[:, None])[:, None, None, None, :]
    cache_scores = soft_cap(
        jnp.einsum("prgjd,pcgd->prgjc", prompt_queries, cache_k, preferred_element_type=jnp.float32)
    )
    prefix_part = partial_softmax(cache_scores, cache_allowed, cache_v, "prgjc,pcgd->prgjd")
    prefix_part = (
        prefix_part[0].reshape(dec_total, kv_heads, group_size),
        prefix_part[1].reshape(dec_total, kv_heads, group_size, HEAD),
    )
    slot_count = tail_keys.shape[0]
    tail_len = tail_keys.shape[1]
    sample_total = tail_slots.shape[0]
    local_slots = seq_index * slot_count + jnp.arange(slot_count, dtype=jnp.int32)
    owner = tail_slots[None, :] == local_slots[:, None]
    slot_queries = jnp.dot(
        owner.astype(jnp.bfloat16),
        dec_query.reshape(sample_total, NEW * q_heads * HEAD),
        preferred_element_type=jnp.float32,
    )
    slot_queries = slot_queries.astype(jnp.bfloat16).reshape(
        slot_count, NEW, kv_heads, group_size, HEAD
    )
    slot_lengths = jnp.sum(jnp.where(owner, tail_lengths[None, :], 0), axis=1)
    tail_allowed = (jnp.arange(tail_len, dtype=jnp.int32)[None, :] < slot_lengths[:, None])[
        :, None, None, None, :
    ]
    slot_keys = tail_keys.reshape(slot_count, tail_len, kv_heads, HEAD)
    slot_values = tail_values.reshape(slot_count, tail_len, kv_heads, HEAD)
    tail_scores = soft_cap(
        jnp.einsum("sngjd,stgd->sngjt", slot_queries, slot_keys, preferred_element_type=jnp.float32)
    )
    slot_part = partial_softmax(tail_scores, tail_allowed, slot_values, "sngjt,stgd->sngjd")
    owned_by = owner.T
    tail_sum = jnp.sum(jnp.where(owned_by[:, :, None, None, None], slot_part[0][None], 0.0), axis=1)
    tail_mix = jnp.sum(
        jnp.where(owned_by[:, :, None, None, None, None], slot_part[1][None], 0.0), axis=1
    )
    tail_part = (
        tail_sum.reshape(dec_total, kv_heads, group_size),
        tail_mix.reshape(dec_total, kv_heads, group_size, HEAD),
    )
    partials = combine(prefix_part, tail_part)
    combined = combined_all(partials, "seq", combine)
    merged = tuple(
        (lax.dynamic_slice_in_dim(member, seq_index * dec_rows, dec_rows, 0) for member in combined)
    )
    own_rows = seq_index * dec_rows + jnp.arange(dec_rows, dtype=jnp.int32)
    own_query = lax.dynamic_slice_in_dim(dec_query, seq_index * dec_rows, dec_rows, 0).reshape(
        dec_rows, kv_heads, group_size, HEAD
    )
    near_ids = (own_rows // NEW)[:, None] * NEW + jnp.arange(NEW, dtype=jnp.int32)[None, :]
    near_keys = jnp.take(dec_key, near_ids, axis=0).reshape(dec_rows, NEW, kv_heads, HEAD)
    near_values = jnp.take(dec_value, near_ids, axis=0).reshape(dec_rows, NEW, kv_heads, HEAD)
    near_allowed = (jnp.arange(NEW, dtype=jnp.int32)[None, :] <= (own_rows % NEW)[:, None])[
        :, None, None, :
    ]
    near_scores = soft_cap(
        jnp.einsum("rgjd,rmgd->rgjm", own_query, near_keys, preferred_element_type=jnp.float32)
    )
    near_part = partial_softmax(near_scores, near_allowed, near_values, "rgjm,rmgd->rgjd")
    finished = combine(merged, near_part)
    dec_attn = (
        (finished[1] / finished[0][..., None])
        .astype(jnp.bfloat16)
        .reshape(dec_rows, q_heads * HEAD)
    )
    attn_rows = jnp.concatenate([pf_attn, dec_attn], axis=0)
    heads_all = lax.all_gather(attn_rows, "tp", axis=1, tiled=True)
    columns = heads_all
    projected = jnp.dot(
        columns,
        lax.all_gather(w_output, "seq", axis=0, tiled=True),
        preferred_element_type=jnp.float32,
    )
    projected = projected.astype(jnp.bfloat16)
    return (projected[:pf_rows], projected[pf_rows:])


def solution(mesh):
    return jax.shard_map(
        shards,
        mesh=mesh,
        in_specs=(
            P("seq", None),
            P(),
            P(),
            P("seq", "tp"),
            P("seq", "tp"),
            P("seq", "tp"),
            P("seq", "tp"),
            P(),
            P(),
            P(),
            P(),
            P(None, "seq", "tp"),
            P(None, "seq", "tp"),
            P("seq", None, "tp"),
            P("seq", None, "tp"),
        ),
        out_specs=(P("seq", "tp"), P("seq", "tp")),
        check_vma=False,
    )
```

profile of v0, /device:TPU:2, one launch (start us, length us, event | category | flops | bytes accessed | tf_op | source)
XLA Modules:
  0.0 830.4 jit_solution(975228371402905375)
XLA Ops:
  7.2 0.7 all-gather.15.cloned.1.call-update
  8.0 0.7 all-gather.9.cloned.1.call-update
  8.7 0.7 all-gather.13.cloned.1.call-update
  9.5 2.5 fusion.4
  12.0 94.7 %all-gather.15.cloned.1.call-done = bf16[4608,256]{1,0:T(8,128)(2,1)} async-done(((bf16[144,256]{1,0:T(8,128)(2,1)}), bf16[4608,256]{1,0:T(8,128)(2,1)}) %all-gather.15.cloned.1.call-update) | async-done | bytes 2359312 | tf_op jit(solution)/shard_map/all_gather | solution.py:125
  106.7 2.6 convolution_convert_fusion.1
  109.4 0.7 slice.87
  111.3 86.3 %all-gather.9.cloned.1.call-done = bf16[4608,256]{1,0:T(8,128)(2,1)} async-done(((bf16[144,256]{1,0:T(8,128)(2,1)}), bf16[4608,256]{1,0:T(8,128)(2,1)}) %all-gather.9.cloned.1.call-update) | async-done | bytes 2359312 | tf_op jit(solution)/shard_map/all_gather | solution.py:124
  197.6 2.8 fusion.58
  201.5 0.8 copy.156
  202.4 1.7 reshape.524
  204.1 1.7 reshape.528
  205.8 1.7 reshape.532
  207.5 1.7 reshape.530
  210.2 101.4 %all-gather.13.cloned.1.call-done = bf16[4608,512]{1,0:T(8,128)(2,1)} async-done(((bf16[144,512]{1,0:T(8,128)(2,1)}), bf16[4608,512]{1,0:T(8,128)(2,1)}) %all-gather.13.cloned.1.call-update) | async-done | bytes 4718608 | tf_op jit(solution)/shard_map/all_gather | solution.py:123
  311.6 5.1 fusion.56
  316.7 1.3 reshape.520
  321.3 0.7 all-gather.23.cloned.1.call-update
  326.4 102.9 %all_gather.34 = bf16[32,64,2,2]{1,3,2,0:T(2,128)(2,1)S(1)} all-gather(bf16[1,64,2,2]{1,3,2,0:T(2,128)(2,1)S(1)} %add_convert_fusion.2), channel_id=1, replica_groups=mesh['seq'=32,'tp'=8] {'seq'}, dimensions={0}, use_global_device_ids=true | all-gather | bytes 16896 | tf_op jit(solution)/shard_map/all_gather | solution.py:18
  429.6 6.4 copy.159
  436.0 108.2 %all-gather.11.cloned.1.call-done = bf16[8192,256]{0,1:T(8,128)(2,1)} async-done(((bf16[256,256]{0,1:T(8,128)(2,1)}), bf16[8192,256]{0,1:T(8,128)(2,1)}) %all-gather.11.cloned.1.call-update) | async-done | bytes 4194320 | tf_op jit(solution)/shard_map/all_gather | solution.py:149
  544.3 14.0 %while.34 = (s32[]{:T(128)}, f32[256,2,2]{0,2,1:T(2,128)S(1)}, f32[256,2,2,128]{3,0,2,1:T(8,128)S(1)}, s32[]{:T(128)}, s32[]{:T(128)}, /*index=5*/s32[256]{0:T(2...) while((s32[]{:T(128)}, f32[256,2,2]{0,2,1:T(2,128)S(1)}, ...), condition=%wide.region_12.13_spmd.clone, body=%wide.region_6.12_spmd.clone.sunk | while | flops 271590688 | bytes 5275049 | solution.py:187
  547.7 3.1 conditional.3
  547.7 1.1 constant_dynamic-slice_fusion
  549.3 0.9 fusion.60
  558.6 74.9 %all-gather.19.cloned.1.call-done = bf16[32,64,2,2,128]{4,1,3,2,0:T(8,128)(2,1)} async-done(((bf16[1,64,2,2,128]{4,1,3,2,0:T(8,128)(2,1)}), bf16[32,64,2,2,128]{4,1,3,2,0:T(8,128)(2,1)}) %all-gather.19.cloned.1.call-update) | async-done | bytes 2097168 | tf_op jit(solution)/shard_map/all_gather | solution.py:18
  633.5 0.8 fusion.31
  634.4 33.7 %while.33 = (s32[]{:T(128)}, f32[64,2,2]{0,2,1:T(2,128)S(1)}, f32[64,2,2,128]{3,2,1,0:T(2,128)S(1)}, bf16[32,64,2,2]{1,3,2,0:T(2,128)(2,1)S(1)}, bf16[32,64,2,2,...) while((s32[]{:T(128)}, f32[64,2,2]{0,2,1:T(2,128)S(1)}, f32[64,2,2,128]{3,2,1,0:T(2,128)S(1)}, ...), condition=%wide.region_19.20_spmd, body=%wide.region_18.19_spmd.sunk | while | flops 66053 | bytes 461447 | solution.py:26
  634.5 0.9 constant_dynamic-slice_fusion.5
  635.5 0.9 constant_dynamic-slice_fusion.5
  636.6 0.9 constant_dynamic-slice_fusion.5
  637.7 0.9 constant_dynamic-slice_fusion.5
  638.8 0.9 constant_dynamic-slice_fusion.5
  639.9 0.9 constant_dynamic-slice_fusion.5
  641.0 0.9 constant_dynamic-slice_fusion.5
  642.1 0.9 constant_dynamic-slice_fusion.5
  643.1 0.9 constant_dynamic-slice_fusion.5
  644.2 0.9 constant_dynamic-slice_fusion.5
  645.3 0.9 constant_dynamic-slice_fusion.5
  646.4 0.9 constant_dynamic-slice_fusion.5
  647.5 0.9 constant_dynamic-slice_fusion.5
  648.6 0.9 constant_dynamic-slice_fusion.5
  649.7 0.9 constant_dynamic-slice_fusion.5
  650.8 0.9 constant_dynamic-slice_fusion.5
  651.8 0.9 constant_dynamic-slice_fusion.5
  652.9 0.9 constant_dynamic-slice_fusion.5
  654.0 0.9 constant_dynamic-slice_fusion.5
  655.1 0.9 constant_dynamic-slice_fusion.5
  656.2 0.9 constant_dynamic-slice_fusion.5
  657.3 0.9 constant_dynamic-slice_fusion.5
  658.4 0.9 constant_dynamic-slice_fusion.5
  659.5 0.9 constant_dynamic-slice_fusion.5
  660.5 0.9 constant_dynamic-slice_fusion.5
  661.6 0.9 constant_dynamic-slice_fusion.5
  662.7 0.9 constant_dynamic-slice_fusion.5
  663.8 0.9 constant_dynamic-slice_fusion.5
  664.9 0.9 constant_dynamic-slice_fusion.5
  666.0 0.9 constant_dynamic-slice_fusion.5
  667.1 0.9 constant_dynamic-slice_fusion.5
  668.7 0.8 pad_maximum_fusion.1
  669.5 104.2 %all-gather.23.cloned.1.call-done = bf16[4096,576]{0,1:T(8,128)(2,1)} async-done(((bf16[128,576]{0,1:T(8,128)(2,1)}), bf16[4096,576]{0,1:T(8,128)(2,1)}) %all-gather.23.cloned.1.call-update) | async-done | bytes 4718608 | tf_op jit(solution)/shard_map/all_gather | solution.py:271
  773.7 42.5 %all-gather.21.cloned.1.call-done = bf16[258,4096]{0,1:T(8,128)(2,1)} async-done(((bf16[258,512]{0,1:T(8,128)(2,1)}), bf16[258,4096]{0,1:T(8,128)(2,1)}) %all-gather.21.cloned.1.call-update) | async-done | bytes 2113552 | tf_op jit(solution)/shard_map/all_gather | solution.py:267
  816.1 5.9 convolution_convert_fusion
  822.7 0.9 copy.180
  (211 shorter events, 20.1 us)
Async XLA Ops:
  7.2 99.5 %copy-start.2 = (bf16[64,4608]{1,0:T(8,128)(2,1)S(1)}, bf16[64,4608]{1,0:T(8,128)(2,1)}, u32[]{:S(2)}) copy-start(bf16[64,4608]{1,0:T(8,128)(2,1)} %param.24) | copy-start | bytes 1769476
  7.2 99.5 %copy-start = (bf16[256,4608]{1,0:T(8,128)(2,1)S(1)}, bf16[256,4608]{1,0:T(8,128)(2,1)}, u32[]{:S(2)}) copy-start(bf16[256,4608]{1,0:T(8,128)(2,1)} %param.23) | copy-start | bytes 7077892
  7.2 99.5 %copy-start.10 = (f32[4608]{0:T(1024)S(1)}, f32[4608]{0:T(1024)}, u32[]{:S(2)}) copy-start(f32[4608]{0:T(1024)} %param.25) | copy-start | bytes 55300
  7.2 99.5 %all-gather.15.cloned.1.call-start = ((), (), s32[]{:S(2)}) async-start(), calls=%async_computation.3 | async-start | bytes 2433024 | tf_op jit(solution)/shard_map/all_gather | solution.py:125
  7.9 189.6 %all-gather.9.cloned.1.call-start = ((), (), s32[]{:S(2)}) async-start(), calls=%async_computation | async-start | bytes 2433024 | tf_op jit(solution)/shard_map/all_gather | solution.py:124
  8.7 302.9 %all-gather.13.cloned.1.call-start = ((), (), s32[]{:S(2)}) async-start(), calls=%async_computation.2 | async-start | bytes 4866048 | tf_op jit(solution)/shard_map/all_gather | solution.py:123
  9.4 420.2 %all-gather.17.cloned.1.call-start = ((), (), s32[]{:S(2)}) async-start(), calls=%async_computation.4 | async-start | bytes 4325376 | tf_op jit(solution)/shard_map/all_gather | solution.py:150
  12.0 98.1 %copy-start.9 = (s32[6]{0:T(128)S(1)}, s32[6]{0:T(128)}, u32[]{:S(2)}) copy-start(s32[6]{0:T(128)} %param.30) | copy-start | bytes 76
  12.0 98.3 %copy-start.6 = (s32[2]{0:T(128)S(1)}, s32[2]{0:T(128)}, u32[]{:S(2)}) copy-start(s32[2]{0:T(128)} %param.31) | copy-start | bytes 28
  12.0 98.4 %copy-start.7 = (s32[32]{0:T(128)S(1)}, s32[32]{0:T(128)}, u32[]{:S(2)}) copy-start(s32[32]{0:T(128)} %param.32) | copy-start | bytes 388
  110.0 434.2 %all-gather.11.cloned.1.call-start = ((), (), s32[]{:S(2)}) async-start(), calls=%async_computation.1 | async-start | bytes 4325376 | tf_op jit(solution)/shard_map/all_gather | solution.py:149
  200.4 9.4 %copy-start.8 = (s32[32]{0:T(128)S(1)}, s32[32]{0:T(128)}, u32[]{:S(2)}) copy-start(s32[32]{0:T(128)} %param.33) | copy-start | bytes 388
  202.3 431.1 %all-gather.19.cloned.1.call-start = ((), (), s32[]{:S(2)}) async-start(), calls=%async_computation.5 | async-start | bytes 2162688 | tf_op jit(solution)/shard_map/all_gather | solution.py:18
  318.4 1.0 copy-start.5
  318.4 1.2 copy-start.4
  318.4 1.6 copy-start.3
  318.5 1.9 copy-start.1
  318.6 4.8 copy-start.11
  321.2 452.4 %all-gather.23.cloned.1.call-start = ((), (), s32[]{:S(2)}) async-start(), calls=%async_computation.7 | async-start | bytes 4866048 | tf_op jit(solution)/shard_map/all_gather | solution.py:271
  322.0 494.1 %all-gather.21.cloned.1.call-start = ((), (), s32[]{:S(2)}) async-start(), calls=%async_computation.6 | async-start | bytes 3538944 | tf_op jit(solution)/shard_map/all_gather | solution.py:267
Sparse Core Ops, SparseCore 0:
  11.4 95.2 all-gather.14
  110.1 87.4 all-gather.8
  201.0 110.5 all-gather.12
  314.9 105.5 all-gather.16
  423.6 120.6 all-gather.10
  548.1 85.2 all-gather.18
  636.7 136.9 all-gather.22
  775.5 40.6 all-gather.20
where the time goes:
time: 833 us; the launch traced here: 830 us
  waiting for transfers between devices  615 us (74%)
  blocking collectives  103 us (12%)
  local copies, waits for them, and re-layouts  49.4 us (6%)
  matrix products  19.5 us (2%)
  other arithmetic  16.4 us (2%)
  between operations  15.8 us (2%)
  loops' own time  11.1 us (1%)
    all_gather x1, waiting for transfers between devices, shards(): key_piece = lax.all_gather(pf_key, 'seq', axis=0, tiled=True)  108 us
    all_gather x1, waiting for transfers between devices, shards(): lax.all_gather(w_output, 'seq', axis=0, tiled=True)  104 us
    all_gather x1, blocking collectives, combined_all(): lax.all_gather(part.astype(kind), axis)  103 us
    all_gather x1, waiting for transfers between devices, shards(): lax.all_gather(w_query, 'seq', axis=0, tiled=True)  101 us
    all_gather x1, waiting for transfers between devices, shards(): lax.all_gather(w_value, 'seq', axis=0, tiled=True)  94.7 us
    all_gather x1, waiting for transfers between devices, shards(): lax.all_gather(w_key, 'seq', axis=0, tiled=True)  86.3 us
    all_gather x1, waiting for transfers between devices, combined_all(): lax.all_gather(part.astype(kind), axis)  74.9 us
    all_gather x1, waiting for transfers between devices, shards(): heads_all = lax.all_gather(attn_rows, 'tp', axis=1, tiled=True)  42.5 us
  transfers between devices with their start and end apart: 8, of which 7 were waited for; matrix products, arithmetic and copies ran while one was open for 9% of the time, Pallas kernels for 0%

commit v1 on v0

--- a/solution.py
+++ b/solution.py
@@ -121,7 +121,9 @@
     row_total = normed.shape[0]
     pieces = (
         lax.all_gather(w_query, "seq", axis=0, tiled=True),
-        lax.all_gather(w_key, "seq", axis=0, tiled=True),
+        jnp.concatenate(
+            lax.all_to_all(jnp.stack([w_key] * lax.axis_size("seq")), "seq", 0, 0), axis=0
+        ),
         lax.all_gather(w_value, "seq", axis=0, tiled=True),
     )
     columns = normed

time: 833 us -> 774 us (0.929)
  waiting for transfers between devices: 615 us -> 546 us
    all_gather x1 -> x0, waiting for transfers between devices: 86.3 us -> none  [shards(): lax.all_gather(w_key, 'seq', axis=0, tiled=True)]
    all_to_all x0 -> x1, waiting for transfers between devices: none -> 28.9 us  [shards(): lax.all_to_all(jnp.stack([w_key] * lax.axis_size('seq')), 'seq', 0, 0)]
    all_gather x1, waiting for transfers between devices: 101 us -> 89.4 us  [shards(): lax.all_gather(w_query, 'seq', axis=0, tiled=True)]
  transfers between devices with their start and end apart: 8 -> 8, of which waited for: 7 -> 7; matrix products, arithmetic and copies ran while one was open for 9% -> 11% of each run, Pallas kernels for 0% -> 0%
where the time goes in v1:
time: 774 us; the launch traced here: 772 us
  waiting for transfers between devices  546 us (71%)
  blocking collectives  103 us (13%)
  local copies, waits for them, and re-layouts  51.1 us (7%)
  matrix products  20.1 us (3%)
  other arithmetic  18.8 us (2%)
  between operations  15.9 us (2%)
  loops' own time  10.4 us (1%)
    all_gather x1, waiting for transfers between devices, shards(): key_piece = lax.all_gather(pf_key, 'seq', axis=0, tiled=True)  108 us
    all_gather x1, waiting for transfers between devices, shards(): lax.all_gather(w_output, 'seq', axis=0, tiled=True)  104 us
    all_gather x1, blocking collectives, combined_all(): lax.all_gather(part.astype(kind), axis)  103 us
    all_gather x1, waiting for transfers between devices, shards(): lax.all_gather(w_value, 'seq', axis=0, tiled=True)  95.4 us
    all_gather x1, waiting for transfers between devices, shards(): lax.all_gather(w_query, 'seq', axis=0, tiled=True)  89.4 us
    all_gather x1, waiting for transfers between devices, combined_all(): lax.all_gather(part.astype(kind), axis)  75.6 us
    all_gather x1, waiting for transfers between devices, shards(): heads_all = lax.all_gather(attn_rows, 'tp', axis=1, tiled=True)  42.5 us
    all_to_all x1, waiting for transfers between devices, shards(): lax.all_to_all(jnp.stack([w_key] * lax.axis_size('seq')), 'seq', 0, 0)  28.9 us
  transfers between devices with their start and end apart: 8, of which 7 were waited for; matrix products, arithmetic and copies ran while one was open for 11% of the time, Pallas kernels for 0%

profile of v1, /device:TPU:2, one launch (start us, length us, event | category | flops | bytes accessed | tf_op | source)
XLA Modules:
  0.0 771.9 jit_solution(4925697310129615887)
XLA Ops:
  8.7 2.5 fusion.4
  11.3 95.4 %all-gather.12.cloned.1.call-done = bf16[4608,256]{1,0:T(8,128)(2,1)} async-done(((bf16[144,256]{1,0:T(8,128)(2,1)}), bf16[4608,256]{1,0:T(8,128)(2,1)}) %all-gather.12.cloned.1.call-update) | async-done | bytes 2359312 | tf_op jit(solution)/shard_map/all_gather | solution.py:127
  106.7 2.6 convolution_convert_fusion.1
  110.1 1.6 stack.2
  111.7 6.2 all-to-all-start
  119.2 28.9 %all-to-all-done = bf16[32,144,256]{2,1,0:T(8,128)(2,1)S(1)} async-done(((bf16[32,144,256]{2,1,0:T(8,128)(2,1)}), bf16[32,144,256]{2,1,0:T(8,128)(2,1)S(1)}, u32[]{:S(2)}, u32[]{:S(2)}) %all-to-all-start) | async-done | bytes 2359328 | tf_op jit(solution)/shard_map/all_to_all | solution.py:125
  148.1 2.5 copy.167
  150.6 3.4 fusion.7
  154.3 0.8 copy.168
  155.2 0.8 reshape.528
  155.9 1.7 reshape.532
  157.6 1.0 reshape.536
  158.7 1.0 reshape.534
  160.3 0.8 fusion.47
  162.4 1.2 broadcast_compare_fusion
  163.7 89.4 %all-gather.10.cloned.1.call-done = bf16[4608,512]{1,0:T(8,128)(2,1)} async-done(((bf16[144,512]{1,0:T(8,128)(2,1)}), bf16[4608,512]{1,0:T(8,128)(2,1)}) %all-gather.10.cloned.1.call-update) | async-done | bytes 4718608 | tf_op jit(solution)/shard_map/all_gather | solution.py:123
  253.1 5.1 fusion.59
  258.2 1.3 reshape.524
  267.8 103.1 %all_gather.30 = bf16[32,64,2,2]{1,3,2,0:T(2,128)(2,1)S(1)} all-gather(bf16[1,64,2,2]{1,3,2,0:T(2,128)(2,1)S(1)} %add_convert_fusion.2), channel_id=1, replica_groups=mesh['seq'=32,'tp'=8] {'seq'}, dimensions={0}, use_global_device_ids=true | all-gather | bytes 16896 | tf_op jit(solution)/shard_map/all_gather | solution.py:18
  371.2 6.4 copy.171
  377.6 108.3 %all-gather.8.cloned.1.call-done = bf16[8192,256]{0,1:T(8,128)(2,1)} async-done(((bf16[256,256]{0,1:T(8,128)(2,1)}), bf16[8192,256]{0,1:T(8,128)(2,1)}) %all-gather.8.cloned.1.call-update) | async-done | bytes 4194320 | tf_op jit(solution)/shard_map/all_gather | solution.py:151
  485.9 13.3 %while.34 = (s32[]{:T(128)}, f32[256,2,2]{0,2,1:T(2,128)S(1)}, f32[256,2,2,128]{3,0,2,1:T(8,128)S(1)}, s32[]{:T(128)}, s32[]{:T(128)}, /*index=5*/s32[256]{0:T(2...) while((s32[]{:T(128)}, f32[256,2,2]{0,2,1:T(2,128)S(1)}, ...), condition=%wide.region_12.13_spmd.clone, body=%wide.region_6.12_spmd.clone.sunk | while | flops 271590688 | bytes 5275049 | solution.py:189
  489.1 3.1 conditional.3
  489.1 1.1 constant_dynamic-slice_fusion
  490.7 0.9 fusion.62
  499.4 75.6 %all-gather.16.cloned.1.call-done = bf16[32,64,2,2,128]{4,1,3,2,0:T(8,128)(2,1)} async-done(((bf16[1,64,2,2,128]{4,1,3,2,0:T(8,128)(2,1)}), bf16[32,64,2,2,128]{4,1,3,2,0:T(8,128)(2,1)}) %all-gather.16.cloned.1.call-update) | async-done | bytes 2097168 | tf_op jit(solution)/shard_map/all_gather | solution.py:18
  575.0 0.8 fusion.33
  576.0 33.7 %while.33 = (s32[]{:T(128)}, f32[64,2,2]{0,2,1:T(2,128)S(1)}, f32[64,2,2,128]{3,2,1,0:T(2,128)S(1)}, bf16[32,64,2,2]{1,3,2,0:T(2,128)(2,1)S(1)}, bf16[32,64,2,2,...) while((s32[]{:T(128)}, f32[64,2,2]{0,2,1:T(2,128)S(1)}, f32[64,2,2,128]{3,2,1,0:T(2,128)S(1)}, ...), condition=%wide.region_19.20_spmd, body=%wide.region_18.19_spmd.sunk | while | flops 66053 | bytes 461447 | solution.py:26
  576.0 0.9 constant_dynamic-slice_fusion.5
  577.1 0.9 constant_dynamic-slice_fusion.5
  578.2 0.9 constant_dynamic-slice_fusion.5
  579.3 0.9 constant_dynamic-slice_fusion.5
  580.4 0.9 constant_dynamic-slice_fusion.5
  581.5 0.9 constant_dynamic-slice_fusion.5
  582.6 0.9 constant_dynamic-slice_fusion.5
  583.6 0.9 constant_dynamic-slice_fusion.5
  584.7 0.9 constant_dynamic-slice_fusion.5
  585.8 0.9 constant_dynamic-slice_fusion.5
  586.9 0.9 constant_dynamic-slice_fusion.5
  588.0 0.9 constant_dynamic-slice_fusion.5
  589.1 0.9 constant_dynamic-slice_fusion.5
  590.2 0.9 constant_dynamic-slice_fusion.5
  591.3 0.9 constant_dynamic-slice_fusion.5
  592.3 0.9 constant_dynamic-slice_fusion.5
  593.4 0.9 constant_dynamic-slice_fusion.5
  594.5 0.9 constant_dynamic-slice_fusion.5
  595.6 0.9 constant_dynamic-slice_fusion.5
  596.7 0.9 constant_dynamic-slice_fusion.5
  597.8 0.9 constant_dynamic-slice_fusion.5
  598.9 0.9 constant_dynamic-slice_fusion.5
  600.0 0.9 constant_dynamic-slice_fusion.5
  601.0 0.9 constant_dynamic-slice_fusion.5
  602.1 0.9 constant_dynamic-slice_fusion.5
  603.2 0.9 constant_dynamic-slice_fusion.5
  604.3 0.9 constant_dynamic-slice_fusion.5
  605.4 0.9 constant_dynamic-slice_fusion.5
  606.5 0.9 constant_dynamic-slice_fusion.5
  607.6 0.9 constant_dynamic-slice_fusion.5
  608.6 0.9 constant_dynamic-slice_fusion.5
  610.2 0.8 pad_maximum_fusion.1
  611.1 104.0 %all-gather.20.cloned.1.call-done = bf16[4096,576]{0,1:T(8,128)(2,1)} async-done(((bf16[128,576]{0,1:T(8,128)(2,1)}), bf16[4096,576]{0,1:T(8,128)(2,1)}) %all-gather.20.cloned.1.call-update) | async-done | bytes 4718608 | tf_op jit(solution)/shard_map/all_gather | solution.py:273
  715.1 42.5 %all-gather.18.cloned.1.call-done = bf16[258,4096]{0,1:T(8,128)(2,1)} async-done(((bf16[258,512]{0,1:T(8,128)(2,1)}), bf16[258,4096]{0,1:T(8,128)(2,1)}) %all-gather.18.cloned.1.call-update) | async-done | bytes 2113552 | tf_op jit(solution)/shard_map/all_gather | solution.py:269
  757.6 5.9 convolution_convert_fusion
  764.1 0.9 copy.193
  (229 shorter events, 22.8 us)
Async XLA Ops:
  7.2 99.5 %copy-start.2 = (bf16[64,4608]{1,0:T(8,128)(2,1)S(1)}, bf16[64,4608]{1,0:T(8,128)(2,1)}, u32[]{:S(2)}) copy-start(bf16[64,4608]{1,0:T(8,128)(2,1)} %param.24) | copy-start | bytes 1769476
  7.2 99.5 %copy-start = (bf16[256,4608]{1,0:T(8,128)(2,1)S(1)}, bf16[256,4608]{1,0:T(8,128)(2,1)}, u32[]{:S(2)}) copy-start(bf16[256,4608]{1,0:T(8,128)(2,1)} %param.23) | copy-start | bytes 7077892
  7.2 99.5 %copy-start.18 = (f32[4608]{0:T(1024)S(1)}, f32[4608]{0:T(1024)}, u32[]{:S(2)}) copy-start(f32[4608]{0:T(1024)} %param.25) | copy-start | bytes 55300
  7.2 99.5 %all-gather.12.cloned.1.call-start = ((), (), s32[]{:S(2)}) async-start(), calls=%async_computation.3 | async-start | bytes 2433024 | tf_op jit(solution)/shard_map/all_gather | solution.py:127
  7.9 245.1 %all-gather.10.cloned.1.call-start = ((), (), s32[]{:S(2)}) async-start(), calls=%async_computation.2 | async-start | bytes 4866048 | tf_op jit(solution)/shard_map/all_gather | solution.py:123
  8.7 362.5 %all-gather.14.cloned.1.call-start = ((), (), s32[]{:S(2)}) async-start(), calls=%async_computation.4 | async-start | bytes 4325376 | tf_op jit(solution)/shard_map/all_gather | solution.py:152
  11.3 139.3 %copy-start.8 = (f32[320]{0:T(512)}, f32[320]{0:T(512)S(1)}, u32[]{:S(2)}) copy-start(f32[320]{0:T(512)S(1)} %add_rsqrt_fusion) | copy-start | bytes 3844
  11.3 98.8 %copy-start.7 = (bf16[144,256]{1,0:T(8,128)(2,1)S(1)}, bf16[144,256]{1,0:T(8,128)(2,1)}, u32[]{:S(2)}) copy-start(bf16[144,256]{1,0:T(8,128)(2,1)} %param.27) | copy-start | bytes 221188
  109.4 2.4 copy-start.6
  110.1 7.9 %copy-start.16 = (s32[6]{0:T(128)S(1)}, s32[6]{0:T(128)}, u32[]{:S(2)}) copy-start(s32[6]{0:T(128)} %param.30) | copy-start | bytes 76
  110.1 8.1 %copy-start.10 = (s32[2]{0:T(128)S(1)}, s32[2]{0:T(128)}, u32[]{:S(2)}) copy-start(s32[2]{0:T(128)} %param.31) | copy-start | bytes 28
  110.1 8.2 %copy-start.11 = (s32[32]{0:T(128)S(1)}, s32[32]{0:T(128)}, u32[]{:S(2)}) copy-start(s32[32]{0:T(128)} %param.32) | copy-start | bytes 388
  111.7 36.3 %all-to-all-start = ((bf16[32,144,256]{2,1,0:T(8,128)(2,1)}), bf16[32,144,256]{2,1,0:T(8,128)(2,1)S(1)}, u32[]{:S(2)}, u32[]{:S(2)}) async-start(bf16[32,144,256]{2,1,0:T(8,128)(2,1)} %stack.2), calls=%async_computation | async-start | bytes 4718592 | tf_op jit(solution)/shard_map/all_to_all | solution.py:125
  117.9 367.9 %all-gather.8.cloned.1.call-start = ((), (), s32[]{:S(2)}) async-start(), calls=%async_computation.1 | async-start | bytes 4325376 | tf_op jit(solution)/shard_map/all_gather | solution.py:151
  150.6 4.6 copy-start.3
  154.0 6.3 copy-start.12
  154.0 99.1 %copy-start.1 = (bf16[256,4608]{1,0:T(8,128)(2,1)S(1)}, bf16[256,4608]{1,0:T(8,128)(2,1)}, u32[]{:S(2)}) copy-start(bf16[256,4608]{1,0:T(8,128)(2,1)} %param.23) | copy-start | bytes 7077892
  155.1 419.9 %all-gather.16.cloned.1.call-start = ((), (), s32[]{:S(2)}) async-start(), calls=%async_computation.5 | async-start | bytes 2162688 | tf_op jit(solution)/shard_map/all_gather | solution.py:18
  160.3 0.8 copy-start.14
  259.9 0.7 copy-start.13
  259.9 0.7 copy-start.15
  259.9 1.0 copy-start.5
  259.9 0.9 copy-start.19
  260.0 1.6 copy-start.4
  260.0 1.6 copy-start.9
  260.1 4.7 copy-start.20
  260.1 6.0 slice-start
  262.8 452.4 %all-gather.20.cloned.1.call-start = ((), (), s32[]{:S(2)}) async-start(), calls=%async_computation.7 | async-start | bytes 4866048 | tf_op jit(solution)/shard_map/all_gather | solution.py:273
  263.3 494.3 %all-gather.18.cloned.1.call-start = ((), (), s32[]{:S(2)}) async-start(), calls=%async_computation.6 | async-start | bytes 3538944 | tf_op jit(solution)/shard_map/all_gather | solution.py:269
  371.2 114.7 %copy-start.17 = (s32[6]{0:T(128)S(1)}, s32[6]{0:T(128)}, u32[]{:S(2)}) copy-start(s32[6]{0:T(128)} %param.30) | copy-start | bytes 76
Sparse Core Ops, SparseCore 0:
  11.4 95.2 all-gather.11
  110.1 142.9 all-gather.9
  256.5 105.5 all-gather.13
  365.2 120.6 all-gather.7
  489.7 85.2 all-gather.15
  578.1 136.9 all-gather.19
  716.9 40.6 all-gather.17
